TPU v7x, 128 devices: a whole 4x4x4 slice. The times are simulated.
128 devices in a mesh: ctx: 16 (over y_lo, z, core), head: 8 (over x, y_hi).
Axes of the slice: x: 4, y: 4 (y_hi: 2, y_lo: 2; y = y_hi * 2 + y_lo), z: 4, core: 2. Of those that a mesh axis runs over, the one named last changes fastest.
Arguments:
- hidden_in: bfloat16 [4096, 8192], P('ctx', 'head'), may hold values from -90 to 90
- query_rows: bfloat16 [4096, 8192], P('ctx', 'head'), may hold values from -5 to 5
- key_rows: bfloat16 [4096, 1024], P('ctx', 'head'), may hold values from -5 to 5
- value_rows: bfloat16 [4096, 1024], P('ctx', 'head'), may hold values from -6 to 6
- out_weight: bfloat16 [8192, 8192], P('head'), may hold values from -0.0625 to 0.0625
- grad_out: bfloat16 [4096, 8192], P('ctx', 'head'), may hold values from -6 to 6
- answer_mask: int32 [4096], P('ctx'), may hold values 0 or 1
Outputs:
- grad_query: bfloat16 [4096, 8192], P('ctx', 'head')
- grad_key: bfloat16 [4096, 1024], P('ctx', 'head')
- grad_value: bfloat16 [4096, 1024], P('ctx', 'head')
- fisher_q: float32 [16, 64], P('ctx', 'head')
- fisher_o: float32 [16, 64], P('ctx', 'head')
All inputs are finite; a program needn't handle non-finite values. No bound on the sum of `answer_mask` on one device may be relied on, other than what follows from the above.
Results may differ from a plain program's by a relative error of at most 0.019.
Values may be sent and summed in bfloat16 or wider, within the bound.
No kernel may reach another device: no remote copies, remote signals or barrier semaphores. Data moves between devices by JAX's collectives and lax.ppermute only.
A program may use at most 128 MiB of HBM per device.

v0:
```python
import math
import jax
import jax.numpy as jnp
from jax import lax
from jax.sharding import PartitionSpec as P

D = 8192
HEADS = 64
KVH = 8
HD = 128
NEGATIVE = -1e30
EPSILON = 1e-06


def block_scores(query_group, key_block, scaling, row_pos, col_pos):
    scores = (
        jnp.einsum("tgd,kd->tgk", query_group, key_block, preferred_element_type=jnp.float32)
        * scaling
    )
    return jnp.where(row_pos[:, None, None] >= col_pos[None, None, :], scores, NEGATIVE)


def head_squares(left_side, right_side, head_dim):
    product = lax.dot_general(
        left_side, right_side, (((0,), (0,)), ((), ())), preferred_element_type=jnp.float32
    )
    shaped = (product * product).reshape(
        product.shape[0], right_side.shape[1] // head_dim, head_dim
    )
    return jnp.sum(shaped, axis=(0, 2))


def gram_pair_squares(left_gram, right_side, head_dim):
    rows = right_side.shape[0]
    right_heads = right_side.reshape(rows, right_side.shape[1] // head_dim, head_dim)
    right_gram = jnp.einsum(
        "ihd,jhd->hij", right_heads, right_heads, preferred_element_type=jnp.float32
    )
    return jnp.sum(right_gram * left_gram[None], axis=(1, 2))


def gram_squares(left_side, right_side, head_dim):
    left_gram = lax.dot_general(
        left_side, left_side, (((1,), (1,)), ((), ())), preferred_element_type=jnp.float32
    )
    return gram_pair_squares(left_gram, right_side, head_dim)


def body(hidden_in, query_rows, key_rows, value_rows, out_weight, grad_out, answer_mask):
    tok_dev = query_rows.shape[0]
    head_dim = HD
    group_size = HEADS // KVH
    local_groups = key_rows.shape[1] // head_dim
    scaling = head_dim ** (-0.5)
    own_index = lax.axis_index("ctx")
    first_row = own_index * tok_dev
    loss_weight = 0.25 + answer_mask.astype(jnp.float32)
    weighted = (grad_out.astype(jnp.float32) * loss_weight[:, None]).astype(jnp.bfloat16)
    hidden_gram = lax.psum(
        lax.dot_general(
            hidden_in, hidden_in, (((1,), (1,)), ((), ())), preferred_element_type=jnp.float32
        ),
        "head",
    )
    pair_all = lax.all_gather(
        jnp.concatenate([key_rows, value_rows], axis=1), "ctx", axis=0, tiled=True
    )
    kv_width = key_rows.shape[1]
    keys_all, values_all = (pair_all[:, :kv_width], pair_all[:, kv_width:])
    tokens = keys_all.shape[0]
    block_rows = math.gcd(512, tokens)

    def fetch(table, block_number):
        return lax.dynamic_slice_in_dim(table, block_number * block_rows, block_rows, 0)

    def column_pos(block_number):
        return block_number * block_rows + jnp.arange(block_rows, dtype=jnp.int32)

    buffer = jnp.zeros((tokens, 2 * local_groups * head_dim), jnp.float32)
    rows = query_rows.shape[0]
    row_pos = first_row + jnp.arange(rows, dtype=jnp.int32)
    needed = (first_row + rows - 1) // block_rows + 1
    query_heads = query_rows.reshape(rows, local_groups, group_size, head_dim)
    log_totals = []
    shared_head = 0
    query_group = query_heads[:, shared_head]

    def stats_step(block_number, carried):
        running_max, running_sum = carried
        key_block = fetch(keys_all, block_number)
        scores = block_scores(query_group, key_block, scaling, row_pos, column_pos(block_number))
        new_max = jnp.maximum(running_max, jnp.max(scores, axis=-1))
        running_sum = running_sum * jnp.exp(running_max - new_max) + jnp.sum(
            jnp.exp(scores - new_max[..., None]), axis=-1
        )
        return (new_max, running_sum)

    start_max = jnp.full((rows, group_size), NEGATIVE, jnp.float32)
    start_sum = jnp.zeros((rows, group_size), jnp.float32)
    running_max, running_sum = lax.fori_loop(0, needed, stats_step, (start_max, start_sum))
    log_total = running_max + jnp.log(running_sum)

    def value_step(block_number, accumulated):
        key_block = fetch(keys_all, block_number)
        value_block = fetch(values_all, block_number)
        scores = block_scores(query_group, key_block, scaling, row_pos, column_pos(block_number))
        rounded = jnp.exp(scores - log_total[..., None]).astype(jnp.bfloat16)
        return accumulated + jnp.einsum(
            "tgk,kd->tgd", rounded, value_block, preferred_element_type=jnp.float32
        )

    accumulated = lax.fori_loop(
        0, needed, value_step, jnp.zeros((rows, group_size, head_dim), jnp.float32)
    )
    log_totals.append(log_total)
    attended_list = [accumulated.astype(jnp.bfloat16)]
    attended_part = jnp.stack(attended_list, axis=1).reshape(
        rows, local_groups * group_size * head_dim
    )
    log_totals, attended = (log_totals, attended_part)
    piece_part = lax.all_gather(weighted, "head", axis=1, tiled=True)
    grad_sum = lax.dot_general(
        piece_part, out_weight, (((1,), (1,)), ((), ())), preferred_element_type=jnp.float32
    )
    grad_sum, squares_out = (grad_sum, gram_squares(piece_part, attended, head_dim))
    grad_attended, squares_out = (grad_sum.astype(jnp.bfloat16), squares_out)
    backward_buffer = buffer
    rows = query_rows.shape[0]
    backward_row_pos = first_row + jnp.arange(rows, dtype=jnp.int32)
    needed = (first_row + rows - 1) // block_rows + 1
    query_heads = query_rows.reshape(rows, local_groups, group_size, head_dim)
    grad_heads = grad_attended.reshape(rows, local_groups, group_size, head_dim)
    attended_heads = attended.reshape(rows, local_groups, group_size, head_dim)
    shared_head = 0
    backward_query_group = query_heads[:, shared_head]
    grad_group = grad_heads[:, shared_head]
    backward_log_total = log_totals[shared_head]
    row_dot = jnp.sum(
        grad_group.astype(jnp.float32) * attended_heads[:, shared_head].astype(jnp.float32), axis=-1
    )
    key_column = jnp.int32(shared_head * head_dim)
    value_column = jnp.int32((local_groups + shared_head) * head_dim)

    def back_step(block_number, carried):
        query_sum, buffer_now = carried
        key_block = fetch(keys_all, block_number)
        value_block = fetch(values_all, block_number)
        scores = block_scores(
            backward_query_group, key_block, scaling, backward_row_pos, column_pos(block_number)
        )
        softmax = jnp.exp(scores - backward_log_total[..., None])
        rounded = softmax.astype(jnp.bfloat16)
        grad_prob = jnp.einsum(
            "tgd,kd->tgk", grad_group, value_block, preferred_element_type=jnp.float32
        )
        grad_score = (softmax * (grad_prob - row_dot[..., None]) * scaling).astype(jnp.bfloat16)
        query_sum = query_sum + jnp.einsum(
            "tgk,kd->tgd", grad_score, key_block, preferred_element_type=jnp.float32
        )
        key_part = jnp.einsum(
            "tgk,tgd->kd", grad_score, backward_query_group, preferred_element_type=jnp.float32
        )
        value_part = jnp.einsum(
            "tgk,tgd->kd", rounded, grad_group, preferred_element_type=jnp.float32
        )
        row_start = (block_number * block_rows).astype(jnp.int32)
        old_key = lax.dynamic_slice(buffer_now, (row_start, key_column), (block_rows, head_dim))
        buffer_now = lax.dynamic_update_slice(
            buffer_now, old_key + key_part, (row_start, key_column)
        )
        old_value = lax.dynamic_slice(buffer_now, (row_start, value_column), (block_rows, head_dim))
        buffer_now = lax.dynamic_update_slice(
            buffer_now, old_value + value_part, (row_start, value_column)
        )
        return (query_sum, buffer_now)

    start_query = jnp.zeros((rows, group_size, head_dim), jnp.float32)
    query_sum, backward_buffer = lax.fori_loop(0, needed, back_step, (start_query, backward_buffer))
    query_grads = [query_sum.astype(jnp.bfloat16)]
    grad_query_part = jnp.stack(query_grads, axis=1).reshape(
        rows, local_groups * group_size * head_dim
    )
    key_sums = lax.psum_scatter(
        backward_buffer.astype(jnp.bfloat16), "ctx", scatter_dimension=0, tiled=True
    ).astype(jnp.float32)
    grad_key = key_sums[:, : local_groups * head_dim].astype(jnp.bfloat16)
    grad_value = key_sums[:, local_groups * head_dim :].astype(jnp.bfloat16)
    squares_query = gram_pair_squares(hidden_gram, grad_query_part, head_dim)
    normal_size = D * head_dim * tok_dev
    fisher_q = jnp.log(squares_query / normal_size + EPSILON).reshape(1, -1)
    fisher_o = jnp.log(squares_out / normal_size + EPSILON).reshape(1, -1)
    return (grad_query_part, grad_key, grad_value, fisher_q, fisher_o)


def solution(mesh):
    return jax.shard_map(
        body,
        mesh=mesh,
        in_specs=(
            P("ctx", "head"),
            P("ctx", "head"),
            P("ctx", "head"),
            P("ctx", "head"),
            P("head", None),
            P("ctx", "head"),
            P("ctx"),
        ),
        out_specs=(
            P("ctx", "head"),
            P("ctx", "head"),
            P("ctx", "head"),
            P("ctx", "head"),
            P("ctx", "head"),
        ),
        check_vma=False,
    )
```

profile of v0, /device:TPU:0, one launch (start us, length us, event | category | flops | bytes accessed | tf_op | source)
XLA Modules:
  0.0 287.8 jit_solution(4906694200121494240)
XLA Ops:
  7.2 1.6 pad_maximum_fusion
  9.6 2.0 multiply_convert_fusion
  12.8 1.2 copy.18
  14.3 1.1 copy.21
  15.4 31.1 %all-gather.3.cloned.1.call-done = bf16[4096,256]{1,0:T(8,128)(2,1)} async-done(((bf16[256,256]{1,0:T(8,128)(2,1)}), bf16[4096,256]{1,0:T(8,128)(2,1)}) %all-gather.3.cloned.1.call-update) | async-done | bytes 2097168 | tf_op jit(solution)/shard_map/all_gather | solution.py:65
  46.4 2.7 fusion.62
  49.2 1.9 while.37
  51.1 3.0 %while.38 = (s32[]{:T(128)}, f32[256,8,128]{2,0,1:T(8,128)S(1)}, s32[]{:T(128)}, bf16[4096,128]{1,0:T(8,128)(2,1)S(1)}, bf16[256,8,128]{2,1,0:T(8,128)(2,1)}, /*...) while((s32[]{:T(128)}, f32[256,8,128]{2,0,1:T(8,128)S(1)}, ...), condition=%wide.region_5.6_spmd.clone, body=%wide.region_4.5_spmd.clone.sunk | while | flops 541459200 | bytes 3161259 | solution.py:112
  51.3 2.8 fusion.104
  54.1 65.9 %all-gather.5.cloned.1.call-done = bf16[256,8192]{1,0:T(8,128)(2,1)} async-done(((bf16[256,1024]{1,0:T(8,128)(2,1)}), bf16[256,8192]{1,0:T(8,128)(2,1)}) %all-gather.5.cloned.1.call-update) | async-done | bytes 4194320 | tf_op jit(solution)/shard_map/all_gather | solution.py:121
  120.1 12.4 %fusion.59 = bf16[32,8,8,128]{3,2,1,0:T(8,128)(2,1)} fusion(bf16[256,8192]{1,0:T(8,128)(2,1)} %all-gather.5.cloned.1.call-done, bf16[1024,8192]{1,0:T(8,128)(2,1)} %param.17), kind=kOutput, calls=%fused_computation.65 | convolution fusion | flops 4295229440 | bytes 21495808 | tf_op jit(solution)/shard_map/dot_general | solution.py:122
  132.4 1.9 copy.36
  134.4 1.4 multiply_reduce_fusion.2
  135.8 2.2 broadcast_in_dim.50
  138.1 9.5 %while.39 = (s32[]{:T(128)}, f32[256,8,128]{2,0,1:T(8,128)S(1)}, f32[4096,256]{1,0:T(8,128)}, s32[]{:T(128)}, bf16[4096,128]{1,0:T(8,128)(2,1)S(1)}, /*index=5*/...) while((s32[]{:T(128)}, f32[256,8,128]{2,0,1:T(8,128)S(1)}, ...), condition=%wide.region_8.9_spmd.clone, body=%wide.region_7.8_spmd.clone.sunk | while | flops 1354236672 | bytes 27031796 | solution.py:178
  139.1 2.4 fusion.116
  142.5 2.4 fusion.117
  144.9 2.7 fusion.118
  147.6 3.8 %convert_element_type.47 = bf16[4096,256]{1,0:T(8,128)(2,1)} convert(f32[4096,256]{1,0:T(8,128)} %get-tuple-element.150) | non-fusion elementwise | flops 1048576 | bytes 6291456 | tf_op jit(solution)/shard_map/convert_element_type | solution.py:184
  151.4 4.8 %fusion.65 = f32[256,256]{1,0:T(8,128)S(1)} fusion(bf16[256,8192]{1,0:T(8,128)(2,1)} %all-gather.5.cloned.1.call-done), kind=kOutput, calls=%fused_computation.81 | convolution fusion | flops 1073741824 | bytes 4456448 | tf_op jit(solution)/shard_map/dot_general | solution.py:43
  156.8 47.9 %all-reduce.2.cloned.1.call-done = f32[256,256]{1,0:T(8,128)} async-done(((f32[256,256]{1,0:T(8,128)}), f32[256,256]{1,0:T(8,128)}) %all-reduce.2.cloned.1.call-update) | async-done | bytes 262160 | tf_op jit(solution)/shard_map/psum | solution.py:59
  204.7 1.5 multiply_reduce_fusion.1
  208.1 71.6 %reduce-scatter.2.cloned.1.call-done = bf16[256,256]{1,0:T(8,128)(2,1)} async-done(((bf16[4096,256]{1,0:T(8,128)(2,1)}), bf16[256,256]{1,0:T(8,128)(2,1)}) %reduce-scatter.2.cloned.1.call-update) | async-done | bytes 131088 | tf_op jit(solution)/shard_map/reduce_scatter | solution.py:183
  279.7 1.5 fusion.63
  (44 shorter events, 8.8 us)
Async XLA Ops:
  7.2 4.5 %copy-start = (bf16[256,1024]{1,0:T(8,128)(2,1)S(1)}, bf16[256,1024]{1,0:T(8,128)(2,1)}, u32[]{:S(2)}) copy-start(bf16[256,1024]{1,0:T(8,128)(2,1)} %param.13) | copy-start | bytes 1572868
  7.2 39.3 %all-gather.3.cloned.1.call-start = ((), (), s32[]{:S(2)}) async-start(), calls=%async_computation.1 | async-start | bytes 2228224 | tf_op jit(solution)/shard_map/all_gather | solution.py:65
  8.8 111.3 %all-gather.5.cloned.1.call-start = ((), (), s32[]{:S(2)}) async-start(), calls=%async_computation.2 | async-start | bytes 4718592 | tf_op jit(solution)/shard_map/all_gather | solution.py:121
  11.6 193.1 %all-reduce.2.cloned.1.call-start = ((), (), s32[]{:S(2)}) async-start(), calls=%async_computation.4 | async-start | bytes 524288 | tf_op jit(solution)/shard_map/psum | solution.py:59
  12.7 267.0 %reduce-scatter.2.cloned.1.call-start = ((), (), s32[]{:S(2)}) async-start(), calls=%async_computation.3 | async-start | bytes 2228224 | tf_op jit(solution)/shard_map/reduce_scatter | solution.py:183
  54.1 80.2 %copy-start.1 = (f32[256,8,128]{2,0,1:T(8,128)}, f32[256,8,128]{2,0,1:T(8,128)S(1)}, u32[]{:S(2)}) copy-start(f32[256,8,128]{2,0,1:T(8,128)S(1)} %get-tuple-element.148) | copy-start | bytes 3145732
  138.1 1.0 copy-start.3
  151.4 4.8 %copy-start.2 = (f32[256,8,128]{2,0,1:T(8,128)S(1)}, f32[256,8,128]{2,0,1:T(8,128)}, u32[]{:S(2)}) copy-start(f32[256,8,128]{2,0,1:T(8,128)} %copy-done.1) | copy-start | bytes 3145732
Sparse Core Ops, SparseCore 0:
  9.7 36.6 all-gather.2
  48.8 71.2 all-gather.4
  122.6 82.0 all-reduce.1
  207.1 72.5 reduce-scatter.1
where the time goes:
time: 289 us; the launch traced here: 288 us
  waiting for transfers between devices  217 us (75%)
  matrix products  33 us (11%)
  between operations  13.9 us (5%)
  other arithmetic  12.7 us (4%)
  local copies, waits for them, and re-layouts  11.4 us (4%)
    reduce_scatter x1, waiting for transfers between devices, body(): lax.psum_scatter(backward_buffer.astype(jnp.bfloat16), 'ctx', scatter_dim...  71.6 us
    all_gather x1, waiting for transfers between devices, body(): piece_part = lax.all_gather(weighted, 'head', axis=1, tiled=True)  65.9 us
    psum x1, waiting for transfers between devices, body(): lax.psum(lax.dot_general(hidden_in, hidden_in, (((1,), (1,)), ((), ())),...  47.9 us
    all_gather x1, waiting for transfers between devices, body(): lax.all_gather(jnp.concatenate([key_rows, value_rows], axis=1), 'ctx', ax...  31.1 us
    dot_general x1, matrix products, body(): lax.dot_general(piece_part, out_weight, (((1,), (1,)), ((), ())), preferr...  12.4 us
  transfers between devices with their start and end apart: 4, of which 4 were waited for; matrix products, arithmetic and copies ran while one was open for 19% of the time, Pallas kernels for 0%

commit v1 on v0

--- a/solution.py
+++ b/solution.py
@@ -56,12 +56,11 @@
     first_row = own_index * tok_dev
     loss_weight = 0.25 + answer_mask.astype(jnp.float32)
     weighted = (grad_out.astype(jnp.float32) * loss_weight[:, None]).astype(jnp.bfloat16)
-    hidden_gram = lax.psum(
-        lax.dot_general(
-            hidden_in, hidden_in, (((1,), (1,)), ((), ())), preferred_element_type=jnp.float32
-        ),
-        "head",
-    )
+    block = lax.dot_general(
+        hidden_in, hidden_in, (((1,), (1,)), ((), ())), preferred_element_type=jnp.float32
+    )
+    parts = lax.all_gather(block, "head", axis=0, tiled=False)
+    hidden_gram = parts.sum(axis=0)
     pair_all = lax.all_gather(
         jnp.concatenate([key_rows, value_rows], axis=1), "ctx", axis=0, tiled=True
     )

time: 289 us -> 289 us (level)
    psum x1 -> x0, waiting for transfers between devices: 47.9 us -> none  [body(): lax.psum(lax.dot_general(hidden_in, hidden_in, (((1,), (1,)), ((), ())),...]
    all_gather x0 -> x1, waiting for transfers between devices: none -> 24 us  [body(): parts = lax.all_gather(block, 'head', axis=0, tiled=False)]
    reduce_scatter x1, waiting for transfers between devices: 71.6 us -> 95.3 us  [body(): lax.psum_scatter(backward_buffer.astype(jnp.bfloat16), 'ctx', scatter_dim...]
where the time goes in v1:
time: 289 us; the launch traced here: 288 us
  waiting for transfers between devices  216 us (75%)
  matrix products  32 us (11%)
  between operations  13.9 us (5%)
  other arithmetic  13.8 us (5%)
  local copies, waits for them, and re-layouts  11.3 us (4%)
    reduce_scatter x1, waiting for transfers between devices, body(): lax.psum_scatter(backward_buffer.astype(jnp.bfloat16), 'ctx', scatter_dim...  95.3 us
    all_gather x1, waiting for transfers between devices, body(): piece_part = lax.all_gather(weighted, 'head', axis=1, tiled=True)  66 us
    all_gather x1, waiting for transfers between devices, body(): lax.all_gather(jnp.concatenate([key_rows, value_rows], axis=1), 'ctx', ax...  31.1 us
    all_gather x1, waiting for transfers between devices, body(): parts = lax.all_gather(block, 'head', axis=0, tiled=False)  24 us
    dot_general x1, matrix products, body(): lax.dot_general(piece_part, out_weight, (((1,), (1,)), ((), ())), preferr...  12.4 us
  transfers between devices with their start and end apart: 4, of which 4 were waited for; matrix products, arithmetic and copies ran while one was open for 19% of the time, Pallas kernels for 0%

profile of v1, /device:TPU:0, one launch (start us, length us, event | category | flops | bytes accessed | tf_op | source)
XLA Modules:
  0.0 287.8 jit_solution(17035835455614103852)
XLA Ops:
  7.2 1.6 pad_maximum_fusion
  9.6 2.0 multiply_convert_fusion
  12.8 1.2 copy.18
  14.3 1.1 copy.21
  15.4 31.1 %all-gather.5.cloned.1.call-done = bf16[4096,256]{1,0:T(8,128)(2,1)} async-done(((bf16[256,256]{1,0:T(8,128)(2,1)}), bf16[4096,256]{1,0:T(8,128)(2,1)}) %all-gather.5.cloned.1.call-update) | async-done | bytes 2097168 | tf_op jit(solution)/shard_map/all_gather | solution.py:64
  46.4 2.6 fusion.62
  49.1 1.9 while.37
  51.1 3.0 %while.38 = (s32[]{:T(128)}, f32[256,8,128]{2,0,1:T(8,128)S(1)}, s32[]{:T(128)}, bf16[4096,128]{1,0:T(8,128)(2,1)S(1)}, bf16[256,8,128]{2,1,0:T(8,128)(2,1)}, /*...) while((s32[]{:T(128)}, f32[256,8,128]{2,0,1:T(8,128)S(1)}, ...), condition=%wide.region_5.6_spmd.clone, body=%wide.region_4.5_spmd.clone.sunk | while | flops 541459200 | bytes 3161259 | solution.py:111
  51.3 2.8 fusion.104
  54.1 66.0 %all-gather.7.cloned.1.call-done = bf16[256,8192]{1,0:T(8,128)(2,1)} async-done(((bf16[256,1024]{1,0:T(8,128)(2,1)}), bf16[256,8192]{1,0:T(8,128)(2,1)}) %all-gather.7.cloned.1.call-update) | async-done | bytes 4194320 | tf_op jit(solution)/shard_map/all_gather | solution.py:120
  120.1 12.4 %fusion.59 = bf16[32,8,8,128]{3,2,1,0:T(8,128)(2,1)} fusion(bf16[256,8192]{1,0:T(8,128)(2,1)} %all-gather.7.cloned.1.call-done, bf16[1024,8192]{1,0:T(8,128)(2,1)} %param.17), kind=kOutput, calls=%fused_computation.65 | convolution fusion | flops 4295229440 | bytes 21495808 | tf_op jit(solution)/shard_map/dot_general | solution.py:121
  132.5 1.9 copy.36
  134.4 1.4 multiply_reduce_fusion.2
  135.8 2.2 broadcast_in_dim.50
  138.1 9.5 %while.39 = (s32[]{:T(128)}, f32[256,8,128]{2,0,1:T(8,128)S(1)}, f32[4096,256]{1,0:T(8,128)}, s32[]{:T(128)}, bf16[4096,128]{1,0:T(8,128)(2,1)S(1)}, /*index=5*/...) while((s32[]{:T(128)}, f32[256,8,128]{2,0,1:T(8,128)S(1)}, ...), condition=%wide.region_8.9_spmd.clone, body=%wide.region_7.8_spmd.clone.sunk | while | flops 1354236672 | bytes 27031796 | solution.py:177
  139.1 2.4 fusion.116
  142.5 2.4 fusion.117
  144.9 2.7 fusion.118
  147.6 3.7 %convert_element_type.47 = bf16[4096,256]{1,0:T(8,128)(2,1)} convert(f32[4096,256]{1,0:T(8,128)} %get-tuple-element.150) | non-fusion elementwise | flops 1048576 | bytes 6291456 | tf_op jit(solution)/shard_map/convert_element_type | solution.py:183
  151.3 24.0 %all-gather.9.cloned.1.call-done = f32[2048,256]{1,0:T(8,128)} async-done(((f32[256,256]{1,0:T(8,128)}), f32[2048,256]{1,0:T(8,128)}) %all-gather.9.cloned.1.call-update) | async-done | bytes 2097168 | tf_op jit(solution)/shard_map/all_gather | solution.py:62
  175.3 1.8 reduce_sum.46
  177.1 4.8 %fusion.65 = f32[256,256]{1,0:T(8,128)S(1)} fusion(bf16[256,8192]{1,0:T(8,128)(2,1)} %all-gather.7.cloned.1.call-done), kind=kOutput, calls=%fused_computation.81 | convolution fusion | flops 1073741824 | bytes 4456448 | tf_op jit(solution)/shard_map/dot_general | solution.py:43
  184.4 95.3 %reduce-scatter.2.cloned.1.call-done = bf16[256,256]{1,0:T(8,128)(2,1)} async-done(((bf16[4096,256]{1,0:T(8,128)(2,1)}), bf16[256,256]{1,0:T(8,128)(2,1)}) %reduce-scatter.2.cloned.1.call-update) | async-done | bytes 131088 | tf_op jit(solution)/shard_map/reduce_scatter | solution.py:182
  279.7 1.5 fusion.63
  (44 shorter events, 8.8 us)
Async XLA Ops:
  7.2 4.5 %copy-start = (bf16[256,1024]{1,0:T(8,128)(2,1)S(1)}, bf16[256,1024]{1,0:T(8,128)(2,1)}, u32[]{:S(2)}) copy-start(bf16[256,1024]{1,0:T(8,128)(2,1)} %param.13) | copy-start | bytes 1572868
  7.2 39.3 %all-gather.5.cloned.1.call-start = ((), (), s32[]{:S(2)}) async-start(), calls=%async_computation.1 | async-start | bytes 2228224 | tf_op jit(solution)/shard_map/all_gather | solution.py:64
  8.9 111.2 %all-gather.7.cloned.1.call-start = ((), (), s32[]{:S(2)}) async-start(), calls=%async_computation.2 | async-start | bytes 4718592 | tf_op jit(solution)/shard_map/all_gather | solution.py:120
  11.6 163.7 %all-gather.9.cloned.1.call-start = ((), (), s32[]{:S(2)}) async-start(), calls=%async_computation.4 | async-start | bytes 2359296 | tf_op jit(solution)/shard_map/all_gather | solution.py:62
  12.7 267.0 %reduce-scatter.2.cloned.1.call-start = ((), (), s32[]{:S(2)}) async-start(), calls=%async_computation.3 | async-start | bytes 2228224 | tf_op jit(solution)/shard_map/reduce_scatter | solution.py:182
  54.1 80.3 %copy-start.1 = (f32[256,8,128]{2,0,1:T(8,128)}, f32[256,8,128]{2,0,1:T(8,128)S(1)}, u32[]{:S(2)}) copy-start(f32[256,8,128]{2,0,1:T(8,128)S(1)} %get-tuple-element.148) | copy-start | bytes 3145732
  138.1 1.1 copy-start.3
  177.0 4.8 %copy-start.2 = (f32[256,8,128]{2,0,1:T(8,128)S(1)}, f32[256,8,128]{2,0,1:T(8,128)}, u32[]{:S(2)}) copy-start(f32[256,8,128]{2,0,1:T(8,128)} %copy-done.1) | copy-start | bytes 3145732
Sparse Core Ops, SparseCore 0:
  9.7 36.6 all-gather.4
  48.8 71.2 all-gather.6
  122.4 52.8 all-gather.8
  177.5 102.1 reduce-scatter.1
